TPU v7x, 32 devices: a whole 2x2x4 slice. The times are simulated.
32 devices in a mesh: energy: 4 (over z), atom: 8 (over y, x, core).
Axes of the slice: x: 2, y: 2, z: 4, core: 2. Of those that a mesh axis runs over, the one named last changes fastest.
Arguments:
- t_mats: bfloat16 [4, 16, 2048], P('energy', 'atom'), may hold values from -0.75 to 0.75
- struct_table: bfloat16 [4, 64, 2048], P('energy'), may hold values from -0.359375 to 0.359375
- zone_atoms: int32 [16, 64], P('atom'), may hold values from 0 to 15, as said below
- zone_size: int32 [16], P('atom'), may hold values from 32 to 64
- pair_index: int32 [16, 384], P('atom'), may hold values from 0 to 63
- zone_link: int32 [16, 384], P('atom'), may hold values from 0 to 63
- weights: float32 [4, 2], P('energy'), may hold values from -1 to 1
Outputs:
- green: float32 [16, 2048], P('atom')
Inputs may be any that keep to these rules, and one draw needn't show every extreme that they name: Atom g is owned by index g // 2 of the atom axis; zone_atoms[g, 0] is g; the owner of every member of atom g's zone lies -4 to 3 steps from g's owner along the atom axis, counted around the axis, and both extreme offsets occur in every zone; members may repeat (periodic images).
All inputs are finite; a program needn't handle non-finite values.
Results may differ from a plain program's by a relative error of at most 0.003.
Values may be sent and summed in bfloat16 or wider, within the bound.
No kernel may reach another device: no remote copies, remote signals or barrier semaphores. Data moves between devices by JAX's collectives and lax.ppermute only.
A program may use at most 128 MiB of HBM per device.

v0:
```python
import jax
import jax.numpy as jnp
from jax import lax
from jax.sharding import PartitionSpec as P

L = 32
Z = 64
NB = 6


def real_form(block):
    parts = block.reshape(block.shape[:-1] + (2, L, L))
    real_part = parts[..., 0, :, :]
    imag_part = parts[..., 1, :, :]
    top_rows = jnp.concatenate([real_part, -imag_part], axis=-1)
    bottom_rows = jnp.concatenate([imag_part, real_part], axis=-1)
    return jnp.concatenate([top_rows, bottom_rows], axis=-2)


def take_rows(table, index):
    a_dev = index.shape[0]
    return jnp.take_along_axis(table, index.reshape(a_dev, -1), axis=1).reshape(index.shape)


def body(t_mats, struct_table, zone_atoms, zone_size, pair_index, zone_link, weights):
    e_dev, a_dev, block_flat = t_mats.shape
    window = lax.all_gather(t_mats, "atom", axis=1, tiled=True)
    coupling = jnp.arange(NB, dtype=jnp.int32)
    s2 = zone_link[:, :NB]
    s1 = take_rows(zone_link, s2[:, :, None] * NB + coupling)
    n1 = NB * NB
    slots = jnp.concatenate([s1.reshape(a_dev, n1), s2, jnp.zeros((a_dev, 1), jnp.int32)], axis=1)
    spots = slots[:, :, None] * NB + coupling
    pairs = take_rows(pair_index, spots)
    links = take_rows(zone_link, spots)
    members = take_rows(zone_atoms, slots)
    present = slots < zone_size[:, None]
    t_block = jnp.where(present[None, :, :, None], window[:, members], jnp.zeros((), jnp.bfloat16))
    t_real = real_form(t_block)
    g_real = real_form(struct_table[:, pairs])
    start_b = real_form(t_mats)[..., :L]
    start_f = start_b.astype(jnp.float32)
    is_zero = (slots == 0)[None, :, :, None, None]
    p1 = jnp.einsum(
        "easkij,eajc->easkic", g_real[:, :, :n1], start_b, preferred_element_type=jnp.float32
    )
    hit = (links[:, :n1] == 0)[None, :, :, :, None, None]
    coupled1 = jnp.sum(jnp.where(hit, p1, 0.0), axis=3).astype(jnp.bfloat16)
    col1 = jnp.einsum(
        "easij,easjc->easic", t_real[:, :, :n1], coupled1, preferred_element_type=jnp.float32
    ) + jnp.where(is_zero[:, :, :n1], start_f[:, :, None], 0.0)
    near2 = col1.astype(jnp.bfloat16).reshape(e_dev, a_dev, NB, NB, 2 * L, L)
    g2 = g_real[:, :, n1 : n1 + NB]
    coupled2 = jnp.einsum(
        "eamnij,eamnjc->eamic", g2, near2, preferred_element_type=jnp.float32
    ).astype(jnp.bfloat16)
    col2 = jnp.einsum(
        "eamij,eamjc->eamic",
        t_real[:, :, n1 : n1 + NB],
        coupled2,
        preferred_element_type=jnp.float32,
    ) + jnp.where(is_zero[:, :, n1 : n1 + NB], start_f[:, :, None], 0.0)
    near3 = col2.astype(jnp.bfloat16)
    coupled3 = jnp.einsum(
        "eanij,eanjc->eaic", g_real[:, :, n1 + NB], near3, preferred_element_type=jnp.float32
    ).astype(jnp.bfloat16)
    diagonal = (
        jnp.einsum(
            "eaij,eajc->eaic", t_real[:, :, n1 + NB], coupled3, preferred_element_type=jnp.float32
        )
        + start_f
    )
    real_rows = diagonal[:, :, :L, :].reshape(e_dev, a_dev, L * L)
    imag_rows = diagonal[:, :, L:, :].reshape(e_dev, a_dev, L * L)
    w_real = weights[:, 0][:, None, None]
    w_imag = weights[:, 1][:, None, None]
    green_real = jnp.sum(w_real * real_rows - w_imag * imag_rows, axis=0)
    green_imag = jnp.sum(w_real * imag_rows + w_imag * real_rows, axis=0)
    local_green = jnp.concatenate([green_real, green_imag], axis=-1)
    return lax.psum(local_green, "energy")


def solution(mesh):
    return jax.shard_map(
        body,
        mesh=mesh,
        in_specs=(
            P("energy", "atom", None),
            P("energy", None, None),
            P("atom", None),
            P("atom"),
            P("atom", None),
            P("atom", None),
            P("energy", None),
        ),
        out_specs=P("atom", None),
        check_vma=False,
    )
```

profile of v0, /device:TPU:0, one launch (start us, length us, event | category | flops | bytes accessed | tf_op | source)
XLA Modules:
  0.0 100.4 jit_solution(1606972806575443180)
XLA Ops:
  0.0 0.8 slice_bitcast_fusion.6
  0.8 0.1 add.205
  0.9 0.1 add.200
  1.0 0.1 reshape.652
  1.1 2.2 %gather_fusion.2 = s32[72]{0:T(128)S(1)} fusion(s32[2,384]{1,0:T(2,128)} %param.14, s32[72]{0:T(128)S(1)} %reshape.652), kind=kCustom, calls=%fused_computation.4 | custom fusion | bytes 1152 | tf_op jit(solution)/shard_map/jit(take_along_axis)/gather | solution.py:22
  3.3 0.1 reshape.655
  3.4 0.1 add.198
  3.7 0.1 add.215
  3.9 0.1 add.217
  4.1 9.7 %gather_fusion.4 = s32[516]{0:T(1024)S(1)} fusion(s32[2,384]{1,0:T(2,128)} %param.13, s32[516]{0:T(1024)S(1)} %reshape.682), kind=kCustom, calls=%fused_computation.clone | custom fusion | bytes 8256 | tf_op jit(solution)/shard_map/jit(take_along_axis)/gather | solution.py:22
  13.9 7.5 %gather_fusion.5 = s32[516]{0:T(1024)S(1)} fusion(s32[2,384]{1,0:T(2,128)S(1)} %copy-done.1, s32[516]{0:T(1024)S(1)} %reshape.682), kind=kCustom, calls=%fused_computation.1.clone | custom fusion | bytes 8256 | tf_op jit(solution)/shard_map/jit(take_along_axis)/gather | solution.py:22
  21.6 0.1 reshape.614
  21.7 0.1 reshape.608
  21.8 0.1 reshape.646
  22.0 3.4 %gather_fusion.1 = bf16[516,2048]{1,0:T(8,128)(2,1)S(1)} fusion(bf16[64,2048]{1,0:T(8,128)(2,1)S(1)} %bitcast.108, s32[1024]{0:T(1024)S(1)} %pad_clamp_fusion), kind=kCustom, calls=%fused_computation.3 | custom fusion | bytes 4229136 | tf_op jit(solution)/shard_map/gather | solution.py:40
  25.4 9.3 %reshape.609 = bf16[1,2,43,6,2,32,32]{6,5,4,3,2,1,0:T(8,128)(2,1)} reshape(bf16[516,2048]{1,0:T(8,128)(2,1)S(1)} %gather_fusion.1) | data formatting | bytes 4227072 | tf_op jit(solution)/shard_map/reshape | solution.py:12
  34.7 7.3 %slice_bitcast_fusion = (bf16[1,2,43,6,32,32]{5,4,3,2,1,0:T(8,128)(2,1)}, bf16[1,2,43,6,32,32]{5,4,3,2,1,0:T(8,128)(2,1)}) fusion(bf16[1,2,43,6,2,32,32]{6,5,4,3,2,1,0:T(8,128)(2,1)} %reshape.609), kind=kLoop, calls=%fused_computation.14 | loop fusion | bytes 4227072 | tf_op jit(solution)/shard_map/squeeze | solution.py:14
  42.1 1.5 %copy-done.3 = bf16[1,2,43,6,2,32,32]{6,5,4,3,2,1,0:T(8,128)(2,1)S(1)} copy-done((bf16[1,2,43,6,2,32,32]{6,5,4,3,2,1,0:T(8,128)(2,1)S(1)}, bf16[1,2,43,6,2,32,32]{6,5,4,3,2,1,0:T(8,128)(2,1)}, u32[]{:S(2)}) %copy-start.3) | copy-done | bytes 2113560
  43.6 2.5 %fusion.70 = bf16[1,2,43,6,32,32]{5,4,3,2,1,0:T(8,128)(2,1)} fusion(bf16[1,2,43,6,2,32,32]{6,5,4,3,2,1,0:T(8,128)(2,1)S(1)} %copy-done.3), kind=kLoop, calls=%fused_computation.115 | loop fusion | flops 528384 | bytes 2113536 | tf_op jit(solution)/shard_map/neg | solution.py:15
  46.1 0.1 reshape.616
  46.2 0.1 copy.45
  46.3 0.1 copy.44
  46.4 0.1 convert_bitcast_fusion
  46.5 9.5 %select_reduce_fusion = bf16[2,36,64,32]{2,3,1,0:T(8,128)(2,1)S(1)} fusion(pred[2,36,6]{2,1,0:T(8,128)(4,1)S(1)} %slice_compare_fusion, bf16[1,2,43,6,32,32]{5,4,3,2,1,0:T(8,128)(2,1)} %get-tuple-element.13, bf16[1,2,43,6,32,32]{5,4,3,2,1,0:T(8,128)(2,1)} %get-tuple-element.12, bf16[1,2,43,6,32,32]{5,4,3,2,1,0:T(8,128)(2,1)} %fusion.70, ...), kind=kOutput, calls=%fused_computation.13 | convolution fusion | flops 129024000 | bytes 3473840 | tf_op jit(solution)/shard_map/easkij,eajc->easkic/dot_general | solution.py:44
  56.0 0.1 shift-left_or_fusion
  56.1 0.1 reshape.658
  56.2 2.0 %gather_fusion.3 = s32[86]{0:T(128)S(1)} fusion(s32[2,64]{1,0:T(2,128)S(1)} %copy-done.2, s32[86]{0:T(128)S(1)} %reshape.658), kind=kCustom, calls=%fused_computation.5 | custom fusion | bytes 1376 | tf_op jit(solution)/shard_map/jit(take_along_axis)/gather | solution.py:22
  58.2 0.1 gather.23
  58.3 0.1 reshape.636
  58.4 10.7 %all_gather.3 = bf16[1,16,2048]{2,0,1:T(2,128)(2,1)S(1)} all-gather(bf16[1,2,2048]{2,0,1:T(2,128)(2,1)S(1)} %copy.27), channel_id=1, replica_groups=mesh['energy'=4,'atom'=8] {'atom'}, dimensions={1}, use_global_device_ids=true | all-gather | bytes 73728 | tf_op jit(solution)/shard_map/all_gather | solution.py:27
  69.1 0.8 gather_fusion
  69.9 1.1 %reshape.694 = bf16[1,2,43,2,32,32]{5,4,3,2,1,0:T(8,128)(2,1)S(1)} reshape(bf16[86,2048]{1,0:T(8,128)(2,1)S(1)} %gather_fusion) | data formatting | bytes 704512 | tf_op jit(solution)/shard_map/gather | solution.py:38
  71.1 0.2 copy_select_fusion
  71.3 0.3 slice_bitcast_fusion.2
  71.6 0.1 fusion.69
  71.7 0.1 add_compare_fusion
  71.8 0.9 fusion.8
  72.8 0.6 copy-done.5
  73.3 1.3 %slice-done.1 = s8[4194304]{0:T(1024)(128)(4,1)S(1)} async-done(((s8[4227072]{0:T(1024)(128)(4,1)}), s8[4194304]{0:T(1024)(128)(4,1)S(1)}, s32[]{:S(2)}) %slice-start.1) | async-done | bytes 4194328
  74.7 1.3 %copy-done.4 = bf16[1,2,43,6,32,32]{5,4,3,2,1,0:T(8,128)(2,1)S(1)} copy-done((bf16[1,2,43,6,32,32]{5,4,3,2,1,0:T(8,128)(2,1)S(1)}, bf16[1,2,43,6,32,32]{5,4,3,2,1,0:T(8,128)(2,1)}, u32[]{:S(2)}) %copy-start.4) | copy-done | bytes 1056792
  75.9 0.8 fusion.23
  76.8 1.5 %fusion.27 = bf16[2,64,32]{1,2,0:T(8,128)(2,1)S(1)} fusion(bf16[2,6,64,32]{2,3,1,0:T(8,128)(2,1)S(1)} %fusion.23, bf16[1,2,43,32,32]{4,3,2,1,0:T(8,128)(2,1)S(1)} %get-tuple-element.15, bf16[1,2,43,32,32]{4,3,2,1,0:T(8,128)(2,1)S(1)} %get-tuple-element.14, bf16[1,2,43,32,32]{4,3,2,1,0:T(8,128)(2,1)S(1)} %fusion.69, ...), kind=kOutput, calls=%fused_computation.41 | convolution fusion | flops 7155712 | bytes 3772428 | tf_op jit(solution)/shard_map/eanij,eanjc->eaic/dot_general | solution.py:64
  78.2 0.2 fusion.26
  78.5 0.6 fusion.73
  79.1 1.4 %multiply_subtract_fusion = (f32[1,2,32,32]{2,3,1,0:T(8,128)S(1)}, f32[1,2,32,32]{2,3,1,0:T(8,128)S(1)}) fusion(f32[1,2,64,32]{2,3,1,0:T(8,128)S(1)} %fusion.26, f32[]{:T(128)} %bitcast.32, f32[]{:T(128)} %bitcast), kind=kLoop, calls=%fused_computation.75 | loop fusion | flops 12288 | bytes 32776 | tf_op jit(solution)/shard_map/sub | solution.py:77
  80.5 0.1 add.226
  80.7 0.1 sub.10
  80.8 19.6 %psum.7 = f32[2,2048]{1,0:T(2,128)} all-reduce(f32[2,2048]{1,0:T(2,128)S(1)} %pad_maximum_fusion.8), channel_id=1, replica_groups=mesh['energy'=4,'atom'=8] {'energy'}, use_global_device_ids=true, to_apply=%region_1.0 | all-reduce | flops 4096 | bytes 32768 | tf_op jit(solution)/shard_map/psum | solution.py:80
  (48 shorter events, 1.1 us)
Async XLA Ops:
  0.0 22.0 %copy-start = (bf16[1,64,2048]{2,1,0:T(8,128)(2,1)S(1)}, bf16[1,64,2048]{2,1,0:T(8,128)(2,1)}, u32[]{:S(2)}) copy-start(bf16[1,64,2048]{2,1,0:T(8,128)(2,1)} %param.10) | copy-start | bytes 786436
  0.0 13.9 %copy-start.1 = (s32[2,384]{1,0:T(2,128)S(1)}, s32[2,384]{1,0:T(2,128)}, u32[]{:S(2)}) copy-start(s32[2,384]{1,0:T(2,128)} %param.14) | copy-start | bytes 9220
  34.7 8.9 %copy-start.3 = (bf16[1,2,43,6,2,32,32]{6,5,4,3,2,1,0:T(8,128)(2,1)S(1)}, bf16[1,2,43,6,2,32,32]{6,5,4,3,2,1,0:T(8,128)(2,1)}, u32[]{:S(2)}) copy-start(bf16[1,2,43,6,2,32,32]{6,5,4,3,2,1,0:T(8,128)(2,1)} %reshape.609) | copy-start | bytes 6340612
  43.6 2.5 %copy-start.6 = (bf16[1,2,2048]{2,1,0:T(2,128)(2,1)S(1)}, bf16[1,2,2048]{2,1,0:T(2,128)(2,1)}, u32[]{:S(2)}) copy-start(bf16[1,2,2048]{2,1,0:T(2,128)(2,1)} %param.9) | copy-start | bytes 24580
  46.5 9.7 %copy-start.2 = (s32[2,64]{1,0:T(2,128)S(1)}, s32[2,64]{1,0:T(2,128)}, u32[]{:S(2)}) copy-start(s32[2,64]{1,0:T(2,128)} %param.11) | copy-start | bytes 1540
  56.0 15.1 %copy-start.8 = (s32[2]{0:T(128)S(1)}, s32[2]{0:T(128)}, u32[]{:S(2)}) copy-start(s32[2]{0:T(128)} %param.12) | copy-start | bytes 28
  69.9 2.8 %slice-start = ((s8[4227072]{0:T(1024)(128)(4,1)}), s8[32768]{0:T(1024)(128)(4,1)S(1)}, s32[]{:S(2)}) async-start(s8[4227072]{0:T(1024)(128)(4,1)} %bitcast.110), calls=%async_computation | async-start | bytes 65536
  71.1 2.2 %copy-start.5 = (bf16[1,2,43,6,32,32]{5,4,3,2,1,0:T(8,128)(2,1)S(1)}, bf16[1,2,43,6,32,32]{5,4,3,2,1,0:T(8,128)(2,1)}, u32[]{:S(2)}) copy-start(bf16[1,2,43,6,32,32]{5,4,3,2,1,0:T(8,128)(2,1)} %get-tuple-element.13) | copy-start | bytes 3170308
  71.3 3.3 %slice-start.1 = ((s8[4227072]{0:T(1024)(128)(4,1)}), s8[4194304]{0:T(1024)(128)(4,1)S(1)}, s32[]{:S(2)}) async-start(s8[4227072]{0:T(1024)(128)(4,1)} %bitcast.110), calls=%async_computation.1 | async-start | bytes 8388608
  71.6 4.3 %copy-start.4 = (bf16[1,2,43,6,32,32]{5,4,3,2,1,0:T(8,128)(2,1)S(1)}, bf16[1,2,43,6,32,32]{5,4,3,2,1,0:T(8,128)(2,1)}, u32[]{:S(2)}) copy-start(bf16[1,2,43,6,32,32]{5,4,3,2,1,0:T(8,128)(2,1)} %get-tuple-element.12) | copy-start | bytes 3170308
  76.8 1.7 %copy-start.7 = (f32[1,2]{1,0:T(1,128)S(1)}, f32[1,2]{1,0:T(1,128)}, u32[]{:S(2)}) copy-start(f32[1,2]{1,0:T(1,128)} %param.15) | copy-start | bytes 28
where the time goes:
time: 101 us; the launch traced here: 100 us
  local copies, waits for them, and re-layouts  51.6 us (51%)
  blocking collectives  30.3 us (30%)
  matrix products  12.9 us (13%)
  other arithmetic  5.4 us (5%)
    gather x11, local copies, waits for them, and re-layouts, take_rows(): jnp.take_along_axis(table, index.reshape(a_dev, -1), axis=1)  22.1 us
    psum x1, blocking collectives, body(): return lax.psum(local_green, 'energy')  19.6 us
    all_gather x1, blocking collectives, body(): window = lax.all_gather(t_mats, 'atom', axis=1, tiled=True)  10.7 us
    dot_general x1, matrix products, body(): jnp.einsum('easkij,eajc->easkic', g_real[:, :, :n1], start_b, preferred_e...  9.49 us
    reshape x2, local copies, waits for them, and re-layouts, real_form(): parts = block.reshape(block.shape[:-1] + (2, L, L))  9.42 us
    squeeze x2, local copies, waits for them, and re-layouts, real_form(): imag_part = parts[..., 1, :, :]  7.6 us
    unnamed x26, local copies, waits for them, and re-layouts  4.99 us
    gather x1, local copies, waits for them, and re-layouts, body(): g_real = real_form(struct_table[:, pairs])  3.39 us

commit v1 on v0

--- a/solution.py
+++ b/solution.py
@@ -24,7 +24,12 @@
 
 def body(t_mats, struct_table, zone_atoms, zone_size, pair_index, zone_link, weights):
     e_dev, a_dev, block_flat = t_mats.shape
-    window = lax.all_gather(t_mats, "atom", axis=1, tiled=True)
+    ring = [t_mats]
+    for hop in range(7):
+        ring.append(lax.ppermute(ring[-1], "atom", [(dev, (dev + 1) % 8) for dev in range(8)]))
+    window = jnp.roll(
+        jnp.concatenate(ring[::-1], axis=1), (lax.axis_index("atom") + 1) * ring[0].shape[1], axis=1
+    )
     coupling = jnp.arange(NB, dtype=jnp.int32)
     s2 = zone_link[:, :NB]
     s1 = take_rows(zone_link, s2[:, :, None] * NB + coupling)

time: 101 us -> 114 us (1.13)
  waiting for transfers between devices: 0 us -> 20.6 us
  blocking collectives: 30.3 us -> 20.3 us
  starting transfers between devices: 0 us -> 3.12 us
  local copies, waits for them, and re-layouts: 51.6 us -> 49.4 us
  matrix products: 12.9 us -> 14.4 us
    ppermute x0 -> x7, waiting for transfers between devices: none -> 20.6 us  [body(): lax.ppermute(ring[-1], 'atom', [(dev, (dev + 1) % 8) for dev in range(8)])]
    all_gather x1 -> x0, blocking collectives: 10.7 us -> none  [body(): window = lax.all_gather(t_mats, 'atom', axis=1, tiled=True)]
    ppermute x0 -> x7, starting transfers between devices: none -> 3.12 us  [body(): lax.ppermute(ring[-1], 'atom', [(dev, (dev + 1) % 8) for dev in range(8)])]
    unnamed x26 -> x20, local copies, waits for them, and re-layouts: 4.99 us -> 2.59 us
    dot_general x1, matrix products: 0.75 us -> 2.17 us  [body(): jnp.einsum('eamnij,eamnjc->eamic', g2, near2, preferred_element_type=jnp....]
  transfers between devices with their start and end apart: 0 -> 7, of which waited for: 0 -> 6; matrix products, arithmetic and copies ran while one was open for 0% -> 51% of each run, Pallas kernels for 0% -> 0%
where the time goes in v1:
time: 114 us; the launch traced here: 113 us
  local copies, waits for them, and re-layouts  49.4 us (43%)
  waiting for transfers between devices  20.6 us (18%)
  blocking collectives  20.3 us (18%)
  matrix products  14.4 us (13%)
  other arithmetic  5.23 us (5%)
  starting transfers between devices  3.12 us (3%)
    gather x11, local copies, waits for them, and re-layouts, take_rows(): jnp.take_along_axis(table, index.reshape(a_dev, -1), axis=1)  22.1 us
    ppermute x7, waiting for transfers between devices, body(): lax.ppermute(ring[-1], 'atom', [(dev, (dev + 1) % 8) for dev in range(8)])  20.6 us
    psum x1, blocking collectives, body(): return lax.psum(local_green, 'energy')  20.3 us
    dot_general x1, matrix products, body(): jnp.einsum('easkij,eajc->easkic', g_real[:, :, :n1], start_b, preferred_e...  9.58 us
    reshape x2, local copies, waits for them, and re-layouts, real_form(): parts = block.reshape(block.shape[:-1] + (2, L, L))  9.45 us
    squeeze x2, local copies, waits for them, and re-layouts, real_form(): imag_part = parts[..., 1, :, :]  7.6 us
    gather x1, local copies, waits for them, and re-layouts, body(): g_real = real_form(struct_table[:, pairs])  3.39 us
    ppermute x7, starting transfers between devices, body(): lax.ppermute(ring[-1], 'atom', [(dev, (dev + 1) % 8) for dev in range(8)])  3.12 us
  transfers between devices with their start and end apart: 7, of which 6 were waited for; matrix products, arithmetic and copies ran while one was open for 51% of the time, Pallas kernels for 0%

profile of v1, /device:TPU:0, one launch (start us, length us, event | category | flops | bytes accessed | tf_op | source)
XLA Modules:
  0.0 113.4 jit_solution(326409212958447830)
XLA Ops:
  0.0 0.5 collective-permute-start
  0.5 0.7 slice_bitcast_fusion.6
  1.2 0.1 add.218
  1.5 0.1 reshape.652
  1.6 2.2 %gather_fusion.2 = s32[72]{0:T(128)S(1)} fusion(s32[2,384]{1,0:T(2,128)} %param.14, s32[72]{0:T(128)S(1)} %reshape.652), kind=kCustom, calls=%fused_computation.4 | custom fusion | bytes 1152 | tf_op jit(solution)/shard_map/jit(take_along_axis)/gather | solution.py:22
  3.8 0.1 reshape.655
  4.1 0.1 add.231
  4.2 0.1 add.233
  4.5 9.7 %gather_fusion.5 = s32[516]{0:T(1024)S(1)} fusion(s32[2,384]{1,0:T(2,128)} %param.14, s32[516]{0:T(1024)S(1)} %reshape.682), kind=kCustom, calls=%fused_computation.1.clone | custom fusion | bytes 8256 | tf_op jit(solution)/shard_map/jit(take_along_axis)/gather | solution.py:22
  14.2 7.5 %gather_fusion.4 = s32[516]{0:T(1024)S(1)} fusion(s32[2,384]{1,0:T(2,128)S(1)} %copy-done.1, s32[516]{0:T(1024)S(1)} %reshape.682), kind=kCustom, calls=%fused_computation.clone | custom fusion | bytes 8256 | tf_op jit(solution)/shard_map/jit(take_along_axis)/gather | solution.py:22
  21.8 0.1 reshape.608
  22.0 0.1 reshape.646
  22.1 3.4 %gather_fusion.1 = bf16[516,2048]{1,0:T(8,128)(2,1)S(1)} fusion(bf16[64,2048]{1,0:T(8,128)(2,1)S(1)} %bitcast.107, s32[1024]{0:T(1024)S(1)} %pad_clamp_fusion), kind=kCustom, calls=%fused_computation.3 | custom fusion | bytes 4229136 | tf_op jit(solution)/shard_map/gather | solution.py:45
  25.5 9.4 %reshape.609 = bf16[1,2,43,6,2,32,32]{6,5,4,3,2,1,0:T(8,128)(2,1)} reshape(bf16[516,2048]{1,0:T(8,128)(2,1)S(1)} %gather_fusion.1) | data formatting | bytes 4227072 | tf_op jit(solution)/shard_map/reshape | solution.py:12
  34.9 7.3 %slice_bitcast_fusion = (bf16[1,2,43,6,32,32]{5,4,3,2,1,0:T(8,128)(2,1)}, bf16[1,2,43,6,32,32]{5,4,3,2,1,0:T(8,128)(2,1)}) fusion(bf16[1,2,43,6,2,32,32]{6,5,4,3,2,1,0:T(8,128)(2,1)} %reshape.609), kind=kLoop, calls=%fused_computation.14 | loop fusion | bytes 4227072 | tf_op jit(solution)/shard_map/squeeze | solution.py:14
  42.2 1.5 %copy-done.3 = bf16[1,2,43,6,2,32,32]{6,5,4,3,2,1,0:T(8,128)(2,1)S(1)} copy-done((bf16[1,2,43,6,2,32,32]{6,5,4,3,2,1,0:T(8,128)(2,1)S(1)}, bf16[1,2,43,6,2,32,32]{6,5,4,3,2,1,0:T(8,128)(2,1)}, u32[]{:S(2)}) %copy-start.3) | copy-done | bytes 2113560
  43.8 2.5 %fusion.70 = bf16[1,2,43,6,32,32]{5,4,3,2,1,0:T(8,128)(2,1)} fusion(bf16[1,2,43,6,2,32,32]{6,5,4,3,2,1,0:T(8,128)(2,1)S(1)} %copy-done.3), kind=kLoop, calls=%fused_computation.115 | loop fusion | flops 528384 | bytes 2113536 | tf_op jit(solution)/shard_map/neg | solution.py:15
  46.3 0.1 reshape.616
  46.4 0.1 reshape.614
  46.6 0.1 copy.34
  46.7 0.1 copy.33
  46.9 0.1 reshape.658
  47.0 2.0 %gather_fusion.3 = s32[86]{0:T(128)S(1)} fusion(s32[2,64]{1,0:T(2,128)S(1)} %copy-done.2, s32[86]{0:T(128)S(1)} %reshape.658), kind=kCustom, calls=%fused_computation.5 | custom fusion | bytes 1376 | tf_op jit(solution)/shard_map/jit(take_along_axis)/gather | solution.py:22
  49.0 0.1 gather.23
  49.2 9.6 %select_reduce_fusion = bf16[2,36,64,32]{2,3,1,0:T(8,128)(2,1)S(1)} fusion(pred[2,36,6]{2,1,0:T(8,128)(4,1)S(1)} %slice_compare_fusion, bf16[1,2,43,6,32,32]{5,4,3,2,1,0:T(8,128)(2,1)} %get-tuple-element.13, bf16[1,2,43,6,32,32]{5,4,3,2,1,0:T(8,128)(2,1)} %get-tuple-element.12, bf16[1,2,43,6,32,32]{5,4,3,2,1,0:T(8,128)(2,1)} %fusion.70, ...), kind=kOutput, calls=%fused_computation.13 | convolution fusion | flops 129024000 | bytes 3473840 | tf_op jit(solution)/shard_map/easkij,eajc->easkic/dot_general | solution.py:49
  58.8 2.7 %collective-permute-start.1 = (bf16[1,2,2048]{2,1,0:T(2,128)(2,1)S(1)}, bf16[1,2,2048]{2,1,0:T(2,128)(2,1)S(1)}, u32[]{:S(2)}, u32[]{:S(2)}) collective-permute-start(bf16[1,2,2048]{2,1,0:T(2,128)(2,1)S(1)} %collective-permute-done), channel_id=1, source_target_pairs={{0,1},{1,2},{2,3},{3,4},{4,5},{5,6},{6,7},{7,0},{8,9},{9,10},{10,1... | collective-permute-start | bytes 24584 | tf_op jit(solution)/shard_map/ppermute | solution.py:29
  61.5 1.6 %collective-permute-done.1 = bf16[1,2,2048]{2,1,0:T(2,128)(2,1)S(1)} collective-permute-done((bf16[1,2,2048]{2,1,0:T(2,128)(2,1)S(1)}, bf16[1,2,2048]{2,1,0:T(2,128)(2,1)S(1)}, u32[]{:S(2)}, u32[]{:S(2)}) %collective-permute-start.1) | collective-permute-done | bytes 8224 | tf_op jit(solution)/shard_map/ppermute | solution.py:29
  63.2 3.9 %collective-permute-done.2 = bf16[1,2,2048]{2,1,0:T(2,128)(2,1)S(1)} collective-permute-done((bf16[1,2,2048]{2,1,0:T(2,128)(2,1)S(1)}, bf16[1,2,2048]{2,1,0:T(2,128)(2,1)S(1)}, u32[]{:S(2)}, u32[]{:S(2)}) %collective-permute-start.2) | collective-permute-done | bytes 8224 | tf_op jit(solution)/shard_map/ppermute | solution.py:29
  67.1 4.0 %collective-permute-done.3 = bf16[1,2,2048]{2,1,0:T(2,128)(2,1)S(1)} collective-permute-done((bf16[1,2,2048]{2,1,0:T(2,128)(2,1)S(1)}, bf16[1,2,2048]{2,1,0:T(2,128)(2,1)S(1)}, u32[]{:S(2)}, u32[]{:S(2)}) %collective-permute-start.3) | collective-permute-done | bytes 8224 | tf_op jit(solution)/shard_map/ppermute | solution.py:29
  71.1 3.9 %collective-permute-done.4 = bf16[1,2,2048]{2,1,0:T(2,128)(2,1)S(1)} collective-permute-done((bf16[1,2,2048]{2,1,0:T(2,128)(2,1)S(1)}, bf16[1,2,2048]{2,1,0:T(2,128)(2,1)S(1)}, u32[]{:S(2)}, u32[]{:S(2)}) %collective-permute-start.4) | collective-permute-done | bytes 8224 | tf_op jit(solution)/shard_map/ppermute | solution.py:29
  75.0 0.6 fusion.73
  75.7 3.3 %collective-permute-done.5 = bf16[1,2,2048]{2,1,0:T(2,128)(2,1)S(1)} collective-permute-done((bf16[1,2,2048]{2,1,0:T(2,128)(2,1)S(1)}, bf16[1,2,2048]{2,1,0:T(2,128)(2,1)S(1)}, u32[]{:S(2)}, u32[]{:S(2)}) %collective-permute-start.5) | collective-permute-done | bytes 8224 | tf_op jit(solution)/shard_map/ppermute | solution.py:29
  79.0 3.9 %collective-permute-done.6 = bf16[1,2,2048]{2,1,0:T(2,128)(2,1)S(1)} collective-permute-done((bf16[1,2,2048]{2,1,0:T(2,128)(2,1)S(1)}, bf16[1,2,2048]{2,1,0:T(2,128)(2,1)S(1)}, u32[]{:S(2)}, u32[]{:S(2)}) %collective-permute-start.6) | collective-permute-done | bytes 8224 | tf_op jit(solution)/shard_map/ppermute | solution.py:29
  83.0 0.2 concatenate.105
  83.2 0.8 gather_fusion
  84.1 1.1 reshape.694
  85.2 0.2 copy_select_fusion
  85.4 0.3 slice_bitcast_fusion.2
  85.6 0.1 fusion.69
  85.7 1.0 fusion.8
  86.7 0.8 slice-done.1
  87.5 2.2 %fusion.23 = bf16[2,6,64,32]{2,3,1,0:T(8,128)(2,1)S(1)} fusion(bf16[2,6,6,64,32]{3,4,2,1,0:T(8,128)(2,1)S(1)} %bitcast.110, bf16[1,2,43,6,32,32]{5,4,3,2,1,0:T(8,128)(2,1)} %get-tuple-element.13, bf16[1,2,43,6,32,32]{5,4,3,2,1,0:T(8,128)(2,1)} %get-tuple-element.12, bf16[1,2,43,6,32,32]{5,4,3,2,1,0:T(8,128)(2,1)S(1)} %bitcast.109), kind=kOutput, calls=%fused_computation.36 | convolution fusion | flops 21258240 | bytes 3514368 | tf_op jit(solution)/shard_map/eamnij,eamnjc->eamic/dot_general | solution.py:59
  89.7 1.5 %fusion.27 = bf16[2,64,32]{1,2,0:T(8,128)(2,1)S(1)} fusion(bf16[2,6,64,32]{2,3,1,0:T(8,128)(2,1)S(1)} %fusion.23, bf16[1,2,43,32,32]{4,3,2,1,0:T(8,128)(2,1)S(1)} %get-tuple-element.15, bf16[1,2,43,32,32]{4,3,2,1,0:T(8,128)(2,1)S(1)} %get-tuple-element.14, bf16[1,2,43,32,32]{4,3,2,1,0:T(8,128)(2,1)S(1)} %fusion.69, ...), kind=kOutput, calls=%fused_computation.41 | convolution fusion | flops 7155712 | bytes 3772428 | tf_op jit(solution)/shard_map/eanij,eanjc->eaic/dot_general | solution.py:69
  91.2 0.2 fusion.26
  91.4 1.3 %multiply_subtract_fusion = (f32[1,2,32,32]{2,3,1,0:T(8,128)S(1)}, f32[1,2,32,32]{2,3,1,0:T(8,128)S(1)}) fusion(f32[1,2,64,32]{2,3,1,0:T(8,128)S(1)} %fusion.26, f32[]{:T(128)} %bitcast.33, f32[]{:T(128)} %bitcast), kind=kLoop, calls=%fused_computation.75 | loop fusion | flops 12288 | bytes 32776 | tf_op jit(solution)/shard_map/sub | solution.py:82
  92.8 0.1 add.242
  92.9 0.1 sub.15
  93.0 20.3 %psum.7 = f32[2,2048]{1,0:T(2,128)} all-reduce(f32[2,2048]{1,0:T(2,128)S(1)} %pad_maximum_fusion.8), channel_id=1, replica_groups=mesh['energy'=4,'atom'=8] {'energy'}, use_global_device_ids=true, to_apply=%region_1.3 | all-reduce | flops 4096 | bytes 32768 | tf_op jit(solution)/shard_map/psum | solution.py:85
  (57 shorter events, 1.5 us)
Async XLA Ops:
  0.0 22.1 %copy-start = (bf16[1,64,2048]{2,1,0:T(8,128)(2,1)S(1)}, bf16[1,64,2048]{2,1,0:T(8,128)(2,1)}, u32[]{:S(2)}) copy-start(bf16[1,64,2048]{2,1,0:T(8,128)(2,1)} %param.10) | copy-start | bytes 786436
  0.0 14.2 %copy-start.1 = (s32[2,384]{1,0:T(2,128)S(1)}, s32[2,384]{1,0:T(2,128)}, u32[]{:S(2)}) copy-start(s32[2,384]{1,0:T(2,128)} %param.13) | copy-start | bytes 9220
  0.0 58.8 %collective-permute-start = (bf16[1,2,2048]{2,1,0:T(2,128)(2,1)}, bf16[1,2,2048]{2,1,0:T(2,128)(2,1)S(1)}, u32[]{:S(2)}, u32[]{:S(2)}) collective-permute-start(bf16[1,2,2048]{2,1,0:T(2,128)(2,1)} %param.9), channel_id=1, source_target_pairs={{0,1},{1,2},{2,3},{3,4},{4,5},{5,6},{6,7},{7,0},{8,9},{9,10},{10,1... | collective-permute-start | bytes 24584 | tf_op jit(solution)/shard_map/ppermute | solution.py:29
  34.9 8.9 %copy-start.3 = (bf16[1,2,43,6,2,32,32]{6,5,4,3,2,1,0:T(8,128)(2,1)S(1)}, bf16[1,2,43,6,2,32,32]{6,5,4,3,2,1,0:T(8,128)(2,1)}, u32[]{:S(2)}) copy-start(bf16[1,2,43,6,2,32,32]{6,5,4,3,2,1,0:T(8,128)(2,1)} %reshape.609) | copy-start | bytes 6340612
  43.8 2.5 %copy-start.4 = (bf16[1,2,2048]{2,1,0:T(2,128)(2,1)S(1)}, bf16[1,2,2048]{2,1,0:T(2,128)(2,1)}, u32[]{:S(2)}) copy-start(bf16[1,2,2048]{2,1,0:T(2,128)(2,1)} %param.9) | copy-start | bytes 24580
  43.8 3.2 %copy-start.2 = (s32[2,64]{1,0:T(2,128)S(1)}, s32[2,64]{1,0:T(2,128)}, u32[]{:S(2)}) copy-start(s32[2,64]{1,0:T(2,128)} %param.11) | copy-start | bytes 1540
  49.2 12.3 %copy-start.6 = (s32[2]{0:T(128)S(1)}, s32[2]{0:T(128)}, u32[]{:S(2)}) copy-start(s32[2]{0:T(128)} %param.12) | copy-start | bytes 28
  49.2 25.9 %copy-start.5 = (f32[1,2]{1,0:T(1,128)S(1)}, f32[1,2]{1,0:T(1,128)}, u32[]{:S(2)}) copy-start(f32[1,2]{1,0:T(1,128)} %param.15) | copy-start | bytes 28
  58.8 4.3 %collective-permute-start.1 = (bf16[1,2,2048]{2,1,0:T(2,128)(2,1)S(1)}, bf16[1,2,2048]{2,1,0:T(2,128)(2,1)S(1)}, u32[]{:S(2)}, u32[]{:S(2)}) collective-permute-start(bf16[1,2,2048]{2,1,0:T(2,128)(2,1)S(1)} %collective-permute-done), channel_id=1, source_target_pairs={{0,1},{1,2},{2,3},{3,4},{4,5},{5,6},{6,7},{7,0},{8,9},{9,10},{10,1... | collective-permute-start | bytes 24584 | tf_op jit(solution)/shard_map/ppermute | solution.py:29
  63.1 4.0 %collective-permute-start.2 = (bf16[1,2,2048]{2,1,0:T(2,128)(2,1)S(1)}, bf16[1,2,2048]{2,1,0:T(2,128)(2,1)S(1)}, u32[]{:S(2)}, u32[]{:S(2)}) collective-permute-start(bf16[1,2,2048]{2,1,0:T(2,128)(2,1)S(1)} %collective-permute-done.1), channel_id=1, source_target_pairs={{0,1},{1,2},{2,3},{3,4},{4,5},{5,6},{6,7},{7,0},{8,9},{9,10},{10,1... | collective-permute-start | bytes 24584 | tf_op jit(solution)/shard_map/ppermute | solution.py:29
  67.1 4.0 %collective-permute-start.3 = (bf16[1,2,2048]{2,1,0:T(2,128)(2,1)S(1)}, bf16[1,2,2048]{2,1,0:T(2,128)(2,1)S(1)}, u32[]{:S(2)}, u32[]{:S(2)}) collective-permute-start(bf16[1,2,2048]{2,1,0:T(2,128)(2,1)S(1)} %collective-permute-done.2), channel_id=1, source_target_pairs={{0,1},{1,2},{2,3},{3,4},{4,5},{5,6},{6,7},{7,0},{8,9},{9,10},{10,1... | collective-permute-start | bytes 24584 | tf_op jit(solution)/shard_map/ppermute | solution.py:29
  71.1 4.0 %collective-permute-start.4 = (bf16[1,2,2048]{2,1,0:T(2,128)(2,1)S(1)}, bf16[1,2,2048]{2,1,0:T(2,128)(2,1)S(1)}, u32[]{:S(2)}, u32[]{:S(2)}) collective-permute-start(bf16[1,2,2048]{2,1,0:T(2,128)(2,1)S(1)} %collective-permute-done.3), channel_id=1, source_target_pairs={{0,1},{1,2},{2,3},{3,4},{4,5},{5,6},{6,7},{7,0},{8,9},{9,10},{10,1... | collective-permute-start | bytes 24584 | tf_op jit(solution)/shard_map/ppermute | solution.py:29
  75.0 4.0 %collective-permute-start.5 = (bf16[1,2,2048]{2,1,0:T(2,128)(2,1)S(1)}, bf16[1,2,2048]{2,1,0:T(2,128)(2,1)S(1)}, u32[]{:S(2)}, u32[]{:S(2)}) collective-permute-start(bf16[1,2,2048]{2,1,0:T(2,128)(2,1)S(1)} %collective-permute-done.4), channel_id=1, source_target_pairs={{0,1},{1,2},{2,3},{3,4},{4,5},{5,6},{6,7},{7,0},{8,9},{9,10},{10,1... | collective-permute-start | bytes 24584 | tf_op jit(solution)/shard_map/ppermute | solution.py:29
  79.0 4.0 %collective-permute-start.6 = (bf16[1,2,2048]{2,1,0:T(2,128)(2,1)S(1)}, bf16[1,2,2048]{2,1,0:T(2,128)(2,1)S(1)}, u32[]{:S(2)}, u32[]{:S(2)}) collective-permute-start(bf16[1,2,2048]{2,1,0:T(2,128)(2,1)S(1)} %collective-permute-done.5), channel_id=1, source_target_pairs={{0,1},{1,2},{2,3},{3,4},{4,5},{5,6},{6,7},{7,0},{8,9},{9,10},{10,1... | collective-permute-start | bytes 24584 | tf_op jit(solution)/shard_map/ppermute | solution.py:29
  84.1 2.6 %slice-start = ((s8[4227072]{0:T(1024)(128)(4,1)}), s8[32768]{0:T(1024)(128)(4,1)S(1)}, s32[]{:S(2)}) async-start(s8[4227072]{0:T(1024)(128)(4,1)} %bitcast.108), calls=%async_computation | async-start | bytes 65536
  85.4 2.2 %slice-start.1 = ((s8[4227072]{0:T(1024)(128)(4,1)}), s8[4194304]{0:T(1024)(128)(4,1)S(1)}, s32[]{:S(2)}) async-start(s8[4227072]{0:T(1024)(128)(4,1)} %bitcast.108), calls=%async_computation.1 | async-start | bytes 8388608
